TPU v7x, 256 devices: a whole 4x4x8 slice. The times are simulated.
256 devices in a mesh: space: 16 (over x_hi, z), chan: 8 (over y, core), dp: 2 (over x_lo).
Axes of the slice: x: 4 (x_hi: 2, x_lo: 2; x = x_hi * 2 + x_lo), y: 4, z: 8, core: 2. Of those that a mesh axis runs over, the one named last changes fastest.
Arguments:
- inputs: bfloat16 [2, 32, 8, 128, 512], P('dp', 'space', None, 'chan'), may hold values from -6 to 6
- cotangent: bfloat16 [2, 32, 8, 128, 512], P('dp', 'space', None, 'chan'), may hold values from -6 to 6
- weight: bfloat16 [27, 128, 128], P(None, 'chan'), may hold values from -0.109375 to 0.109375
Outputs:
- input_grad: bfloat16 [2, 32, 8, 128, 512], P('dp', 'space', None, 'chan')
- weight_grad: float32 [27, 128, 128], P(None, 'chan')
All inputs are finite; a program needn't handle non-finite values.
Results may differ from a plain program's by a relative error of at most 0.001.
Values may be sent and summed in bfloat16 or wider, within the bound.
No kernel may reach another device: no remote copies, remote signals or barrier semaphores. Data moves between devices by JAX's collectives and lax.ppermute only.
A program may use at most 64 MiB of HBM per device.

v0:
```python
import math
import jax
import jax.numpy as jnp
from jax import lax
from jax.sharding import PartitionSpec as P


def from_behind(value, axis, steps):
    count = lax.axis_size(axis)
    initial, last = (max(0, -steps), min(count, count - steps))
    return lax.ppermute(value, axis, [(source, source + steps) for source in range(initial, last)])


def exchange_sum(value, axis, distance):
    count = lax.axis_size(axis)
    return value + lax.ppermute(value, axis, [(i, i ^ distance) for i in range(count)])


def butterfly_sum(value):
    value = exchange_sum(value, "dp", 1)
    for distance in (1, 8, 2, 4):
        value = exchange_sum(value, "space", distance)
    return value


def shift_cells(block, step_z, step_y):
    zero = jnp.zeros((), block.dtype)
    config = ((0, 0, 0), (0, 0, 0), (step_z, -step_z, 0), (0, 0, 0), (step_y, -step_y, 0))
    return lax.pad(block, zero, config)


def local(inputs, cotangent, weight):
    samples, planes, depth, channels, width = inputs.shape
    outputs = weight.shape[2]
    gathered = lax.all_gather(cotangent, "chan", axis=3, tiled=True)
    lower_plane = from_behind(gathered[:, -1:], "space", 1)
    upper_plane = from_behind(gathered[:, :1], "space", -1)
    stacked = jnp.concatenate(
        [shift_cells(inputs, -step_z, -step_y) for step_z in (-1, 0, 1) for step_y in (-1, 0, 1)],
        axis=3,
    )
    accum = jnp.zeros(inputs.shape, jnp.float32)
    groups = []
    for step_x in (-1, 0, 1):
        if step_x == 1:
            slab = jnp.concatenate([lower_plane, gathered[:, : planes - 1]], axis=1)
        elif step_x == -1:
            slab = jnp.concatenate([gathered[:, 1:], upper_plane], axis=1)
        else:
            slab = gathered
        first = 9 * (step_x + 1)
        groups.append(
            jnp.einsum("bxzky,bxzcy->kc", stacked, slab, preferred_element_type=jnp.float32)
        )
        for step_y in (-1, 0, 1):
            kernel = weight[first + step_y + 1 : first + 9 : 3].reshape(3 * channels, outputs)
            product = jnp.einsum(
                "bxzcy,kc->bxzky", slab, kernel, preferred_element_type=jnp.float32
            )
            for place, step_z in enumerate((-1, 0, 1)):
                part = product[:, :, :, place * channels : (place + 1) * channels]
                accum = accum + shift_cells(part, step_z, step_y)
    input_grad = accum.astype(jnp.bfloat16)
    local_grad = jnp.concatenate(groups, axis=0).reshape(27, channels, outputs)
    count = samples * lax.axis_size("dp") * planes * lax.axis_size("space") * depth * width
    scale = 1.0 / math.sqrt(count)
    weight_grad = butterfly_sum(local_grad) * scale
    return (input_grad, weight_grad)


def solution(mesh):
    placed = (
        P("dp", "space", None, "chan", None),
        P("dp", "space", None, "chan", None),
        P(None, "chan", None),
    )
    return jax.shard_map(
        local,
        mesh=mesh,
        in_specs=placed,
        out_specs=(P("dp", "space", None, "chan", None), P(None, "chan", None)),
        check_vma=False,
    )
```

profile of v0, /device:TPU:4, one launch (start us, length us, event | category | flops | bytes accessed | tf_op | source)
XLA Modules:
  0.0 135.7 jit_solution(2542420532690271903)
XLA Ops:
  7.2 0.0 copy-start.1
  7.2 0.0 all-gather.2.cloned.1.call-start
  7.2 0.7 all-gather.2.cloned.1.call-update
  7.9 1.1 fusion.64
  9.0 0.0 copy-start.2
  9.0 1.0 fusion.60
  10.0 1.1 fusion.65
  11.1 1.1 fusion.62
  12.2 0.0 copy-done.1
  12.2 0.1 fusion.63
  12.4 0.1 fusion.66
  12.5 0.1 fusion.67
  12.7 28.0 %all-gather.2.cloned.1.call-done = bf16[1,2,8,128,512]{4,3,2,1,0:T(8,128)(2,1)} async-done(((bf16[1,2,8,16,512]{4,3,2,1,0:T(8,128)(2,1)}), bf16[1,2,8,128,512]{4,3,2,1,0:T(8,128)(2,1)}) %all-gather.2.cloned.1.call-update) | async-done | bytes 2097168 | tf_op jit(solution)/shard_map/all_gather | solution.py:35
  40.7 1.9 %fusion.68 = (bf16[1,1,8,128,512]{4,3,2,1,0:T(8,128)(2,1)S(1)}, bf16[1,1,8,128,512]{4,3,2,1,0:T(8,128)(2,1)S(1)}) fusion(bf16[1,2,8,128,512]{4,3,2,1,0:T(8,128)(2,1)} %all-gather.2.cloned.1.call-done), kind=kLoop, calls=%fused_computation.97 | loop fusion | bytes 4194304 | tf_op jit(solution)/shard_map/slice | solution.py:48
  42.6 5.2 %collective-permute-start = (bf16[1,1,8,128,512]{4,3,2,1,0:T(8,128)(2,1)S(1)}, bf16[1,1,8,128,512]{4,3,2,1,0:T(8,128)(2,1)S(1)}, u32[]{:S(2)}, u32[]{:S(2)}) collective-permute-start(bf16[1,1,8,128,512]{4,3,2,1,0:T(8,128)(2,1)S(1)} %get-tuple-element.3), channel_id=1, source_target_pairs={{16,0},{32,16},{48,32},{64,48},{80,64},{96,80},{112,96},{128,112},... | collective-permute-start | bytes 3145736 | tf_op jit(solution)/shard_map/ppermute | solution.py:11
  47.8 1.9 %collective-permute-start.1 = (bf16[1,1,8,128,512]{4,3,2,1,0:T(8,128)(2,1)S(1)}, bf16[1,1,8,128,512]{4,3,2,1,0:T(8,128)(2,1)S(1)}, u32[]{:S(2)}, u32[]{:S(2)}) collective-permute-start(bf16[1,1,8,128,512]{4,3,2,1,0:T(8,128)(2,1)S(1)} %get-tuple-element.2), channel_id=1, source_target_pairs={{0,16},{16,32},{32,48},{48,64},{64,80},{80,96},{96,112},{112,128},... | collective-permute-start | bytes 3145736 | tf_op jit(solution)/shard_map/ppermute | solution.py:11
  49.7 0.4 fusion.19
  50.1 0.1 fusion.74
  50.3 0.4 fusion.16
  50.7 0.4 fusion.13
  51.1 0.4 fusion.72
  51.5 0.8 fusion.25
  52.3 18.3 %collective-permute-done = bf16[1,1,8,128,512]{4,3,2,1,0:T(8,128)(2,1)S(1)} collective-permute-done((bf16[1,1,8,128,512]{4,3,2,1,0:T(8,128)(2,1)S(1)}, bf16[1,1,8,128,512]{4,3,2,1,0:T(8,128)(2,1)S(1)}, u32[]{:S(2)}, u32[]{:S(2)}) %collective-permute-start) | collective-permute-done | bytes 1048608 | tf_op jit(solution)/shard_map/ppermute | solution.py:11
  70.6 0.8 fusion.22
  71.3 7.1 %collective-permute-done.1 = bf16[1,1,8,128,512]{4,3,2,1,0:T(8,128)(2,1)S(1)} collective-permute-done((bf16[1,1,8,128,512]{4,3,2,1,0:T(8,128)(2,1)S(1)}, bf16[1,1,8,128,512]{4,3,2,1,0:T(8,128)(2,1)S(1)}, u32[]{:S(2)}, u32[]{:S(2)}) %collective-permute-start.1) | collective-permute-done | bytes 1048608 | tf_op jit(solution)/shard_map/ppermute | solution.py:11
  78.4 0.8 fusion.30
  79.2 2.2 %collective-permute-start.2 = (f32[27,16,128]{2,1,0:T(8,128)S(1)}, f32[27,16,128]{2,1,0:T(8,128)S(1)}, u32[]{:S(2)}, u32[]{:S(2)}) collective-permute-start(f32[27,16,128]{2,1,0:T(8,128)S(1)} %bitcast.157), channel_id=1, source_target_pairs={{0,1},{1,0},{2,3},{3,2},{4,5},{5,4},{6,7},{7,6},{8,9},{9,8},{10,11... | collective-permute-start | bytes 663560 | tf_op jit(solution)/shard_map/ppermute | solution.py:16
  81.4 0.4 convolution_bitcast_fusion.4
  81.8 0.4 convolution_bitcast_fusion.5
  82.2 0.4 fusion.69
  82.6 0.4 convolution_bitcast_fusion.1
  83.1 0.4 convolution_bitcast_fusion.2
  83.5 2.5 %collective-permute-done.2 = f32[27,16,128]{2,1,0:T(8,128)S(1)} collective-permute-done((f32[27,16,128]{2,1,0:T(8,128)S(1)}, f32[27,16,128]{2,1,0:T(8,128)S(1)}, u32[]{:S(2)}, u32[]{:S(2)}) %collective-permute-start.2) | collective-permute-done | bytes 221216 | tf_op jit(solution)/shard_map/ppermute | solution.py:16
  86.0 0.1 collective-permute-start.3
  86.1 0.4 fusion.75
  86.5 0.4 convolution_bitcast_fusion.3
  87.0 5.1 %collective-permute-done.3 = f32[27,16,128]{2,1,0:T(8,128)S(1)} collective-permute-done((f32[27,16,128]{2,1,0:T(8,128)S(1)}, f32[27,16,128]{2,1,0:T(8,128)S(1)}, u32[]{:S(2)}, u32[]{:S(2)}) %collective-permute-start.3) | collective-permute-done | bytes 221216 | tf_op jit(solution)/shard_map/ppermute | solution.py:16
  92.1 0.1 collective-permute-start.4
  92.2 0.1 fusion.71
  92.3 0.4 convolution_bitcast_fusion
  92.7 6.9 %collective-permute-done.4 = f32[27,16,128]{2,1,0:T(8,128)S(1)} collective-permute-done((f32[27,16,128]{2,1,0:T(8,128)S(1)}, f32[27,16,128]{2,1,0:T(8,128)S(1)}, u32[]{:S(2)}, u32[]{:S(2)}) %collective-permute-start.4) | collective-permute-done | bytes 221216 | tf_op jit(solution)/shard_map/ppermute | solution.py:16
  99.6 0.1 collective-permute-start.5
  99.7 0.1 fusion.77
  99.8 18.3 %collective-permute-done.5 = f32[27,16,128]{2,1,0:T(8,128)S(1)} collective-permute-done((f32[27,16,128]{2,1,0:T(8,128)S(1)}, f32[27,16,128]{2,1,0:T(8,128)S(1)}, u32[]{:S(2)}, u32[]{:S(2)}) %collective-permute-start.5) | collective-permute-done | bytes 221216 | tf_op jit(solution)/shard_map/ppermute | solution.py:16
  118.2 0.1 collective-permute-start.6
  118.3 3.4 %fusion.59 = bf16[1,2,8,16,512]{4,3,2,1,0:T(8,128)(2,1)} fusion(f32[1,2,8,16,512]{4,3,2,1,0:T(8,128)S(1)} %get-tuple-element.26, f32[1,2,8,16,512]{4,3,2,1,0:T(8,128)S(1)} %get-tuple-element.27, f32[1,2,8,16,512]{4,3,2,1,0:T(8,128)S(1)} %get-tuple-element.25, f32[1,2,8,16,512]{4,3,2,1,0:T(8,128)S(1)} %get-tuple-element.41, ...), kind=kLoop, calls=%fused_computation.77 | loop fusion | flops 3538944 | bytes 14417920 | tf_op jit(solution)/shard_map/convert_element_type | solution.py:63
  121.7 6.4 %collective-permute-done.6 = f32[27,16,128]{2,1,0:T(8,128)S(1)} collective-permute-done((f32[27,16,128]{2,1,0:T(8,128)S(1)}, f32[27,16,128]{2,1,0:T(8,128)S(1)}, u32[]{:S(2)}, u32[]{:S(2)}) %collective-permute-start.6) | collective-permute-done | bytes 221216 | tf_op jit(solution)/shard_map/ppermute | solution.py:16
  128.1 0.7 add_multiply_fusion
  (11 shorter events, 0.2 us)
Async XLA Ops:
  7.2 5.0 %copy-start.1 = (bf16[1,2,8,16,512]{4,3,2,1,0:T(8,128)(2,1)S(1)}, bf16[1,2,8,16,512]{4,3,2,1,0:T(8,128)(2,1)}, u32[]{:S(2)}) copy-start(bf16[1,2,8,16,512]{4,3,2,1,0:T(8,128)(2,1)} %param.3) | copy-start | bytes 786436
  7.2 33.5 %all-gather.2.cloned.1.call-start = ((), (), s32[]{:S(2)}) async-start(), calls=%async_computation | async-start | bytes 2359296 | tf_op jit(solution)/shard_map/all_gather | solution.py:35
  9.0 3.7 %copy-start.2 = (bf16[27,16,128]{2,1,0:T(8,128)(2,1)S(1)}, bf16[27,16,128]{2,1,0:T(8,128)(2,1)}, u32[]{:S(2)}) copy-start(bf16[27,16,128]{2,1,0:T(8,128)(2,1)} %param.5) | copy-start | bytes 331780
  40.7 9.0 %copy-start = (bf16[1,2,8,128,512]{4,3,2,1,0:T(8,128)(2,1)S(1)}, bf16[1,2,8,128,512]{4,3,2,1,0:T(8,128)(2,1)}, u32[]{:S(2)}) copy-start(bf16[1,2,8,128,512]{4,3,2,1,0:T(8,128)(2,1)} %all-gather.2.cloned.1.call-done) | copy-start | bytes 6291460
  42.6 28.0 %collective-permute-start = (bf16[1,1,8,128,512]{4,3,2,1,0:T(8,128)(2,1)S(1)}, bf16[1,1,8,128,512]{4,3,2,1,0:T(8,128)(2,1)S(1)}, u32[]{:S(2)}, u32[]{:S(2)}) collective-permute-start(bf16[1,1,8,128,512]{4,3,2,1,0:T(8,128)(2,1)S(1)} %get-tuple-element.3), channel_id=1, source_target_pairs={{16,0},{32,16},{48,32},{64,48},{80,64},{96,80},{112,96},{128,112},... | collective-permute-start | bytes 3145736 | tf_op jit(solution)/shard_map/ppermute | solution.py:11
  47.8 30.6 %collective-permute-start.1 = (bf16[1,1,8,128,512]{4,3,2,1,0:T(8,128)(2,1)S(1)}, bf16[1,1,8,128,512]{4,3,2,1,0:T(8,128)(2,1)S(1)}, u32[]{:S(2)}, u32[]{:S(2)}) collective-permute-start(bf16[1,1,8,128,512]{4,3,2,1,0:T(8,128)(2,1)S(1)} %get-tuple-element.2), channel_id=1, source_target_pairs={{0,16},{16,32},{32,48},{48,64},{64,80},{80,96},{96,112},{112,128},... | collective-permute-start | bytes 3145736 | tf_op jit(solution)/shard_map/ppermute | solution.py:11
  79.2 6.8 %collective-permute-start.2 = (f32[27,16,128]{2,1,0:T(8,128)S(1)}, f32[27,16,128]{2,1,0:T(8,128)S(1)}, u32[]{:S(2)}, u32[]{:S(2)}) collective-permute-start(f32[27,16,128]{2,1,0:T(8,128)S(1)} %bitcast.157), channel_id=1, source_target_pairs={{0,1},{1,0},{2,3},{3,2},{4,5},{5,4},{6,7},{7,6},{8,9},{9,8},{10,11... | collective-permute-start | bytes 663560 | tf_op jit(solution)/shard_map/ppermute | solution.py:16
  86.0 6.0 %collective-permute-start.3 = (f32[27,16,128]{2,1,0:T(8,128)S(1)}, f32[27,16,128]{2,1,0:T(8,128)S(1)}, u32[]{:S(2)}, u32[]{:S(2)}) collective-permute-start(f32[27,16,128]{2,1,0:T(8,128)S(1)} %add.183), channel_id=1, source_target_pairs={{0,16},{16,0},{32,48},{48,32},{64,80},{80,64},{96,112},{112,96},{1... | collective-permute-start | bytes 663560 | tf_op jit(solution)/shard_map/ppermute | solution.py:16
  92.1 7.5 %collective-permute-start.4 = (f32[27,16,128]{2,1,0:T(8,128)S(1)}, f32[27,16,128]{2,1,0:T(8,128)S(1)}, u32[]{:S(2)}, u32[]{:S(2)}) collective-permute-start(f32[27,16,128]{2,1,0:T(8,128)S(1)} %add.184), channel_id=1, source_target_pairs={{0,128},{16,144},{32,160},{48,176},{64,192},{80,208},{96,224},{112... | collective-permute-start | bytes 663560 | tf_op jit(solution)/shard_map/ppermute | solution.py:16
  99.6 18.6 %collective-permute-start.5 = (f32[27,16,128]{2,1,0:T(8,128)S(1)}, f32[27,16,128]{2,1,0:T(8,128)S(1)}, u32[]{:S(2)}, u32[]{:S(2)}) collective-permute-start(f32[27,16,128]{2,1,0:T(8,128)S(1)} %add.185), channel_id=1, source_target_pairs={{0,32},{16,48},{32,0},{48,16},{64,96},{80,112},{96,64},{112,80},{1... | collective-permute-start | bytes 663560 | tf_op jit(solution)/shard_map/ppermute | solution.py:16
  118.2 9.9 %collective-permute-start.6 = (f32[27,16,128]{2,1,0:T(8,128)S(1)}, f32[27,16,128]{2,1,0:T(8,128)S(1)}, u32[]{:S(2)}, u32[]{:S(2)}) collective-permute-start(f32[27,16,128]{2,1,0:T(8,128)S(1)} %add.186), channel_id=1, source_target_pairs={{0,64},{16,80},{32,96},{48,112},{64,0},{80,16},{96,32},{112,48},{1... | collective-permute-start | bytes 663560 | tf_op jit(solution)/shard_map/ppermute | solution.py:16
Sparse Core Ops, SparseCore 0:
  9.8 30.7 all-gather.1
where the time goes:
time: 136 us
  waiting for transfers between devices  93.1 us (68%)
  between operations  14.3 us (11%)
  starting transfers between devices  9.7 us (7%)
  local copies, waits for them, and re-layouts  8.23 us (6%)
  matrix products  6.09 us (4%)
  other arithmetic  4.23 us (3%)
    ppermute x5, waiting for transfers between devices, exchange_sum(): lax.ppermute(value, axis, [(i, i ^ distance) for i in range(count)])  39.2 us
    all_gather x1, waiting for transfers between devices, local(): gathered = lax.all_gather(cotangent, 'chan', axis=3, tiled=True)  28 us
    ppermute x2, waiting for transfers between devices, from_behind(): lax.ppermute(value, axis, [(source, source + steps) for source in range(i...  25.3 us
    ppermute x2, starting transfers between devices, from_behind(): lax.ppermute(value, axis, [(source, source + steps) for source in range(i...  7.13 us
    unnamed x14, local copies, waits for them, and re-layouts  4.55 us
    dot_general x9, matrix products, local(): jnp.einsum('bxzcy,kc->bxzky', slab, kernel, preferred_element_type=jnp.fl...  3.78 us
    convert_element_type x1, other arithmetic, local(): input_grad = accum.astype(jnp.bfloat16)  3.38 us
  transfers between devices with their start and end apart: 8, of which 8 were waited for; matrix products, arithmetic and copies ran while one was open for 11% of the time, Pallas kernels for 0%

commit v1 on v0

--- a/solution.py
+++ b/solution.py
@@ -3,6 +3,12 @@
 import jax.numpy as jnp
 from jax import lax
 from jax.sharding import PartitionSpec as P
+
+
+def laid_out(parts, dim):
+    parts = jnp.moveaxis(parts, 0, dim)
+    shape = parts.shape
+    return parts.reshape(*shape[:dim], shape[dim] * shape[dim + 1], *shape[dim + 2 :])
 
 
 def from_behind(value, axis, steps):
@@ -32,7 +38,19 @@
 def local(inputs, cotangent, weight):
     samples, planes, depth, channels, width = inputs.shape
     outputs = weight.shape[2]
-    gathered = lax.all_gather(cotangent, "chan", axis=3, tiled=True)
+    size = lax.axis_size("chan")
+    pairs = [(i_2, (i_2 + 1) % size) for i_2 in range(size)]
+    back = [(b, a) for a, b in pairs]
+    lower, upper = ([], [])
+    for step in range(size - 1):
+        if step % 2 == 0:
+            lower.append(lax.ppermute(lower[-1] if lower else cotangent, "chan", pairs))
+        else:
+            upper.append(lax.ppermute(upper[-1] if upper else cotangent, "chan", back))
+    blocks = jnp.stack([*lower[::-1], cotangent, *upper])
+    shift = lax.axis_index("chan") - len(lower)
+    blocks = blocks[(jnp.arange(size) - shift) % size]
+    gathered = laid_out(blocks, 3)
     lower_plane = from_behind(gathered[:, -1:], "space", 1)
     upper_plane = from_behind(gathered[:, :1], "space", -1)
     stacked = jnp.concatenate(

time: 136 us -> 119 us (0.88)
  the two profiles are of different devices: /device:TPU:4 before, /device:TPU:25 now
where the time goes in v1:
time: 119 us; the launch traced here: 118 us
  waiting for transfers between devices  59.4 us (50%)
  starting transfers between devices  29.7 us (25%)
  local copies, waits for them, and re-layouts  17.5 us (15%)
  matrix products  6.07 us (5%)
  other arithmetic  4.77 us (4%)
    ppermute x5, waiting for transfers between devices, exchange_sum(): lax.ppermute(value, axis, [(i, i ^ distance) for i in range(count)])  31.2 us
    ppermute x2, waiting for transfers between devices, from_behind(): lax.ppermute(value, axis, [(source, source + steps) for source in range(i...  20 us
    ppermute x5, starting transfers between devices, exchange_sum(): lax.ppermute(value, axis, [(i, i ^ distance) for i in range(count)])  13.9 us
    ppermute x4, starting transfers between devices, local(): lower.append(lax.ppermute(lower[-1] if lower else cotangent, 'chan', pairs))  12.6 us
    unnamed x37, local copies, waits for them, and re-layouts  11.8 us
    ppermute x4, waiting for transfers between devices, local(): lower.append(lax.ppermute(lower[-1] if lower else cotangent, 'chan', pairs))  8.17 us
    dot_general x9, matrix products, local(): jnp.einsum('bxzcy,kc->bxzky', slab, kernel, preferred_element_type=jnp.fl...  3.77 us
    convert_element_type x1, other arithmetic, local(): input_grad = accum.astype(jnp.bfloat16)  3.32 us
  transfers between devices with their start and end apart: 14, of which 10 were waited for; matrix products, arithmetic and copies ran while one was open for 18% of the time, Pallas kernels for 0%

profile of v1, /device:TPU:25, one launch (start us, length us, event | category | flops | bytes accessed | tf_op | source)
XLA Modules:
  0.0 118.5 jit_solution(1809904890247411965)
XLA Ops:
  0.6 2.2 %collective-permute-start = (bf16[1,2,8,16,512]{4,3,2,1,0:T(8,128)(2,1)}, bf16[1,2,8,16,512]{4,3,2,1,0:T(8,128)(2,1)S(1)}, u32[]{:S(2)}, u32[]{:S(2)}) collective-permute-start(bf16[1,2,8,16,512]{4,3,2,1,0:T(8,128)(2,1)} %param.4), channel_id=1, source_target_pairs={{0,2},{2,4},{4,6},{6,8},{8,10},{10,12},{12,14},{14,0},{1,3},{3,5},... | collective-permute-start | bytes 786440 | tf_op jit(solution)/shard_map/ppermute | solution.py:47
  2.9 1.1 fusion.46
  4.0 1.0 fusion.42
  5.0 1.1 fusion.47
  6.0 1.1 fusion.44
  7.1 3.0 %collective-permute-start.1 = (bf16[1,2,8,16,512]{4,3,2,1,0:T(8,128)(2,1)S(1)}, bf16[1,2,8,16,512]{4,3,2,1,0:T(8,128)(2,1)S(1)}, u32[]{:S(2)}, u32[]{:S(2)}) collective-permute-start(bf16[1,2,8,16,512]{4,3,2,1,0:T(8,128)(2,1)S(1)} %collective-permute-done), channel_id=1, source_target_pairs={{0,2},{2,4},{4,6},{6,8},{8,10},{10,12},{12,14},{14,0},{1,3},{3,5},... | collective-permute-start | bytes 786440 | tf_op jit(solution)/shard_map/ppermute | solution.py:47
  10.4 3.0 %collective-permute-done.1 = bf16[1,2,8,16,512]{4,3,2,1,0:T(8,128)(2,1)S(1)} collective-permute-done((bf16[1,2,8,16,512]{4,3,2,1,0:T(8,128)(2,1)S(1)}, bf16[1,2,8,16,512]{4,3,2,1,0:T(8,128)(2,1)S(1)}, u32[]{:S(2)}, u32[]{:S(2)}) %collective-permute-start.1) | collective-permute-done | bytes 262176 | tf_op jit(solution)/shard_map/ppermute | solution.py:47
  13.4 3.7 %collective-permute-start.2 = (bf16[1,2,8,16,512]{4,3,2,1,0:T(8,128)(2,1)S(1)}, bf16[1,2,8,16,512]{4,3,2,1,0:T(8,128)(2,1)S(1)}, u32[]{:S(2)}, u32[]{:S(2)}) collective-permute-start(bf16[1,2,8,16,512]{4,3,2,1,0:T(8,128)(2,1)S(1)} %collective-permute-done.1), channel_id=1, source_target_pairs={{0,2},{2,4},{4,6},{6,8},{8,10},{10,12},{12,14},{14,0},{1,3},{3,5},... | collective-permute-start | bytes 786440 | tf_op jit(solution)/shard_map/ppermute | solution.py:47
  17.3 3.1 %collective-permute-done.2 = bf16[1,2,8,16,512]{4,3,2,1,0:T(8,128)(2,1)S(1)} collective-permute-done((bf16[1,2,8,16,512]{4,3,2,1,0:T(8,128)(2,1)S(1)}, bf16[1,2,8,16,512]{4,3,2,1,0:T(8,128)(2,1)S(1)}, u32[]{:S(2)}, u32[]{:S(2)}) %collective-permute-start.2) | collective-permute-done | bytes 262176 | tf_op jit(solution)/shard_map/ppermute | solution.py:47
  20.4 3.7 %collective-permute-start.3 = (bf16[1,2,8,16,512]{4,3,2,1,0:T(8,128)(2,1)S(1)}, bf16[1,2,8,16,512]{4,3,2,1,0:T(8,128)(2,1)S(1)}, u32[]{:S(2)}, u32[]{:S(2)}) collective-permute-start(bf16[1,2,8,16,512]{4,3,2,1,0:T(8,128)(2,1)S(1)} %collective-permute-done.2), channel_id=1, source_target_pairs={{0,2},{2,4},{4,6},{6,8},{8,10},{10,12},{12,14},{14,0},{1,3},{3,5},... | collective-permute-start | bytes 786440 | tf_op jit(solution)/shard_map/ppermute | solution.py:47
  24.1 0.6 pad_clamp_fusion
  24.7 0.6 fusion.62
  25.4 2.1 %collective-permute-done.3 = bf16[1,2,8,16,512]{4,3,2,1,0:T(8,128)(2,1)S(1)} collective-permute-done((bf16[1,2,8,16,512]{4,3,2,1,0:T(8,128)(2,1)S(1)}, bf16[1,2,8,16,512]{4,3,2,1,0:T(8,128)(2,1)S(1)}, u32[]{:S(2)}, u32[]{:S(2)}) %collective-permute-start.3) | collective-permute-done | bytes 262176 | tf_op jit(solution)/shard_map/ppermute | solution.py:47
  27.4 0.7 bitcast_dynamic-update-slice_fusion.4
  28.2 0.7 bitcast_dynamic-update-slice_fusion.3
  28.9 0.7 bitcast_dynamic-update-slice_fusion.2
  29.6 0.7 bitcast_dynamic-update-slice_fusion.7
  30.4 0.7 bitcast_dynamic-update-slice_fusion.6
  31.1 0.7 bitcast_dynamic-update-slice_fusion.1
  31.8 0.7 bitcast_dynamic-update-slice_fusion
  32.5 0.7 bitcast_dynamic-update-slice_fusion.5
  33.2 2.4 %gather_fusion = bf16[8,2,8,16,512]{4,3,2,1,0:T(8,128)(2,1)S(1)} fusion(bf16[8,2,8,16,512]{4,3,2,1,0:T(8,128)(2,1)} %bitcast.13, s32[1024]{0:T(1024)} %pad_clamp_fusion), kind=kCustom, calls=%fused_computation | custom fusion | bytes 4194336 | tf_op jit(solution)/shard_map/gather | solution.py:52
  36.1 1.9 %collective-permute-start.8 = (bf16[1,1,8,128,512]{4,3,2,1,0:T(8,128)(2,1)S(1)}, bf16[1,1,8,128,512]{4,3,2,1,0:T(8,128)(2,1)S(1)}, u32[]{:S(2)}, u32[]{:S(2)}) collective-permute-start(bf16[1,1,8,128,512]{4,3,2,1,0:T(8,128)(2,1)S(1)} %get-tuple-element.2), channel_id=1, source_target_pairs={{0,16},{16,32},{32,48},{48,64},{64,80},{80,96},{96,112},{112,128},... | collective-permute-start | bytes 3145736 | tf_op jit(solution)/shard_map/ppermute | solution.py:17
  38.0 1.3 %collective-permute-start.7 = (bf16[1,1,8,128,512]{4,3,2,1,0:T(8,128)(2,1)S(1)}, bf16[1,1,8,128,512]{4,3,2,1,0:T(8,128)(2,1)S(1)}, u32[]{:S(2)}, u32[]{:S(2)}) collective-permute-start(bf16[1,1,8,128,512]{4,3,2,1,0:T(8,128)(2,1)S(1)} %get-tuple-element.3), channel_id=1, source_target_pairs={{16,0},{32,16},{48,32},{64,48},{80,64},{96,80},{112,96},{128,112},... | collective-permute-start | bytes 3145736 | tf_op jit(solution)/shard_map/ppermute | solution.py:17
  39.3 0.4 convolution_bitcast_fusion.3
  39.9 0.6 copy-done.9
  40.4 0.4 convolution_bitcast_fusion.4
  41.3 0.4 fusion.56
  41.7 1.2 %copy-done.2 = bf16[1,2,8,144,512]{4,3,2,1,0:T(8,128)(2,1)S(1)} copy-done((bf16[1,2,8,144,512]{4,3,2,1,0:T(8,128)(2,1)S(1)}, bf16[1,2,8,144,512]{4,3,2,1,0:T(8,128)(2,1)}, u32[]{:S(2)}) %copy-start.2) | copy-done | bytes 2359320
  42.9 0.8 fusion.9
  43.7 16.6 %collective-permute-done.8 = bf16[1,1,8,128,512]{4,3,2,1,0:T(8,128)(2,1)S(1)} collective-permute-done((bf16[1,1,8,128,512]{4,3,2,1,0:T(8,128)(2,1)S(1)}, bf16[1,1,8,128,512]{4,3,2,1,0:T(8,128)(2,1)S(1)}, u32[]{:S(2)}, u32[]{:S(2)}) %collective-permute-start.8) | collective-permute-done | bytes 1048608 | tf_op jit(solution)/shard_map/ppermute | solution.py:17
  60.3 0.8 fusion.12
  61.1 3.4 %collective-permute-done.7 = bf16[1,1,8,128,512]{4,3,2,1,0:T(8,128)(2,1)S(1)} collective-permute-done((bf16[1,1,8,128,512]{4,3,2,1,0:T(8,128)(2,1)S(1)}, bf16[1,1,8,128,512]{4,3,2,1,0:T(8,128)(2,1)S(1)}, u32[]{:S(2)}, u32[]{:S(2)}) %collective-permute-start.7) | collective-permute-done | bytes 1048608 | tf_op jit(solution)/shard_map/ppermute | solution.py:17
  64.5 0.8 fusion.6
  65.3 1.3 %collective-permute-start.9 = (f32[27,16,128]{2,1,0:T(8,128)S(1)}, f32[27,16,128]{2,1,0:T(8,128)S(1)}, u32[]{:S(2)}, u32[]{:S(2)}) collective-permute-start(f32[27,16,128]{2,1,0:T(8,128)S(1)} %bitcast.190), channel_id=1, source_target_pairs={{0,1},{1,0},{2,3},{3,2},{4,5},{5,4},{6,7},{7,6},{8,9},{9,8},{10,11... | collective-permute-start | bytes 663560 | tf_op jit(solution)/shard_map/ppermute | solution.py:22
  68.6 0.4 convolution_bitcast_fusion.2
  69.0 3.0 %collective-permute-done.9 = f32[27,16,128]{2,1,0:T(8,128)S(1)} collective-permute-done((f32[27,16,128]{2,1,0:T(8,128)S(1)}, f32[27,16,128]{2,1,0:T(8,128)S(1)}, u32[]{:S(2)}, u32[]{:S(2)}) %collective-permute-start.9) | collective-permute-done | bytes 221216 | tf_op jit(solution)/shard_map/ppermute | solution.py:22
  72.1 1.7 %collective-permute-start.10 = (f32[27,16,128]{2,1,0:T(8,128)S(1)}, f32[27,16,128]{2,1,0:T(8,128)S(1)}, u32[]{:S(2)}, u32[]{:S(2)}) collective-permute-start(f32[27,16,128]{2,1,0:T(8,128)S(1)} %add.209), channel_id=1, source_target_pairs={{0,16},{16,0},{32,48},{48,32},{64,80},{80,64},{96,112},{112,96},{1... | collective-permute-start | bytes 663560 | tf_op jit(solution)/shard_map/ppermute | solution.py:22
  74.1 0.4 convolution_bitcast_fusion.6
  74.6 3.8 %collective-permute-done.10 = f32[27,16,128]{2,1,0:T(8,128)S(1)} collective-permute-done((f32[27,16,128]{2,1,0:T(8,128)S(1)}, f32[27,16,128]{2,1,0:T(8,128)S(1)}, u32[]{:S(2)}, u32[]{:S(2)}) %collective-permute-start.10) | collective-permute-done | bytes 221216 | tf_op jit(solution)/shard_map/ppermute | solution.py:22
  78.4 6.0 %collective-permute-start.11 = (f32[27,16,128]{2,1,0:T(8,128)S(1)}, f32[27,16,128]{2,1,0:T(8,128)S(1)}, u32[]{:S(2)}, u32[]{:S(2)}) collective-permute-start(f32[27,16,128]{2,1,0:T(8,128)S(1)} %add.210), channel_id=1, source_target_pairs={{0,128},{16,144},{32,160},{48,176},{64,192},{80,208},{96,224},{112... | collective-permute-start | bytes 663560 | tf_op jit(solution)/shard_map/ppermute | solution.py:22
  84.9 3.9 %collective-permute-done.11 = f32[27,16,128]{2,1,0:T(8,128)S(1)} collective-permute-done((f32[27,16,128]{2,1,0:T(8,128)S(1)}, f32[27,16,128]{2,1,0:T(8,128)S(1)}, u32[]{:S(2)}, u32[]{:S(2)}) %collective-permute-start.11) | collective-permute-done | bytes 221216 | tf_op jit(solution)/shard_map/ppermute | solution.py:22
  88.9 1.8 %collective-permute-start.12 = (f32[27,16,128]{2,1,0:T(8,128)S(1)}, f32[27,16,128]{2,1,0:T(8,128)S(1)}, u32[]{:S(2)}, u32[]{:S(2)}) collective-permute-start(f32[27,16,128]{2,1,0:T(8,128)S(1)} %add.211), channel_id=1, source_target_pairs={{0,32},{16,48},{32,0},{48,16},{64,96},{80,112},{96,64},{112,80},{1... | collective-permute-start | bytes 663560 | tf_op jit(solution)/shard_map/ppermute | solution.py:22
  90.8 10.9 %collective-permute-done.12 = f32[27,16,128]{2,1,0:T(8,128)S(1)} collective-permute-done((f32[27,16,128]{2,1,0:T(8,128)S(1)}, f32[27,16,128]{2,1,0:T(8,128)S(1)}, u32[]{:S(2)}, u32[]{:S(2)}) %collective-permute-start.12) | collective-permute-done | bytes 221216 | tf_op jit(solution)/shard_map/ppermute | solution.py:22
  101.7 3.2 %collective-permute-start.13 = (f32[27,16,128]{2,1,0:T(8,128)S(1)}, f32[27,16,128]{2,1,0:T(8,128)S(1)}, u32[]{:S(2)}, u32[]{:S(2)}) collective-permute-start(f32[27,16,128]{2,1,0:T(8,128)S(1)} %add.212), channel_id=1, source_target_pairs={{0,64},{16,80},{32,96},{48,112},{64,0},{80,16},{96,32},{112,48},{1... | collective-permute-start | bytes 663560 | tf_op jit(solution)/shard_map/ppermute | solution.py:22
  104.9 3.3 %fusion.41 = bf16[1,2,8,16,512]{4,3,2,1,0:T(8,128)(2,1)} fusion(f32[1,2,8,16,512]{4,3,2,1,0:T(8,128)S(1)} %get-tuple-element.26, f32[1,2,8,16,512]{4,3,2,1,0:T(8,128)S(1)} %get-tuple-element.27, f32[1,2,8,16,512]{4,3,2,1,0:T(8,128)S(1)} %get-tuple-element.25, f32[1,2,8,16,512]{4,3,2,1,0:T(8,128)S(1)} %get-tuple-element.41, ...), kind=kLoop, calls=%fused_computation.71 | loop fusion | flops 3538944 | bytes 14417920 | tf_op jit(solution)/shard_map/convert_element_type | solution.py:81
  108.2 9.6 %collective-permute-done.13 = f32[27,16,128]{2,1,0:T(8,128)S(1)} collective-permute-done((f32[27,16,128]{2,1,0:T(8,128)S(1)}, f32[27,16,128]{2,1,0:T(8,128)S(1)}, u32[]{:S(2)}, u32[]{:S(2)}) %collective-permute-start.13) | collective-permute-done | bytes 221216 | tf_op jit(solution)/shard_map/ppermute | solution.py:22
  117.8 0.7 add_multiply_fusion
  (50 shorter events, 4.5 us)
Async XLA Ops:
  0.6 9.5 %copy-start = (bf16[1,2,8,16,512]{4,3,2,1,0:T(8,128)(2,1)S(1)}, bf16[1,2,8,16,512]{4,3,2,1,0:T(8,128)(2,1)}, u32[]{:S(2)}) copy-start(bf16[1,2,8,16,512]{4,3,2,1,0:T(8,128)(2,1)} %param.3) | copy-start | bytes 786436
  0.6 6.5 %collective-permute-start = (bf16[1,2,8,16,512]{4,3,2,1,0:T(8,128)(2,1)}, bf16[1,2,8,16,512]{4,3,2,1,0:T(8,128)(2,1)S(1)}, u32[]{:S(2)}, u32[]{:S(2)}) collective-permute-start(bf16[1,2,8,16,512]{4,3,2,1,0:T(8,128)(2,1)} %param.4), channel_id=1, source_target_pairs={{0,2},{2,4},{4,6},{6,8},{8,10},{10,12},{12,14},{14,0},{1,3},{3,5},... | collective-permute-start | bytes 786440 | tf_op jit(solution)/shard_map/ppermute | solution.py:47
  2.9 14.4 %collective-permute-start.4 = (bf16[1,2,8,16,512]{4,3,2,1,0:T(8,128)(2,1)}, bf16[1,2,8,16,512]{4,3,2,1,0:T(8,128)(2,1)S(1)}, u32[]{:S(2)}, u32[]{:S(2)}) collective-permute-start(bf16[1,2,8,16,512]{4,3,2,1,0:T(8,128)(2,1)} %param.4), channel_id=1, source_target_pairs={{2,0},{4,2},{6,4},{8,6},{10,8},{12,10},{14,12},{0,14},{3,1},{5,3},... | collective-permute-start | bytes 786440 | tf_op jit(solution)/shard_map/ppermute | solution.py:49
  3.9 20.8 %copy-start.4 = (bf16[27,16,128]{2,1,0:T(8,128)(2,1)S(1)}, bf16[27,16,128]{2,1,0:T(8,128)(2,1)}, u32[]{:S(2)}) copy-start(bf16[27,16,128]{2,1,0:T(8,128)(2,1)} %param.5) | copy-start | bytes 331780
  7.1 6.3 %collective-permute-start.1 = (bf16[1,2,8,16,512]{4,3,2,1,0:T(8,128)(2,1)S(1)}, bf16[1,2,8,16,512]{4,3,2,1,0:T(8,128)(2,1)S(1)}, u32[]{:S(2)}, u32[]{:S(2)}) collective-permute-start(bf16[1,2,8,16,512]{4,3,2,1,0:T(8,128)(2,1)S(1)} %collective-permute-done), channel_id=1, source_target_pairs={{0,2},{2,4},{4,6},{6,8},{8,10},{10,12},{12,14},{14,0},{1,3},{3,5},... | collective-permute-start | bytes 786440 | tf_op jit(solution)/shard_map/ppermute | solution.py:47
  10.1 20.2 %copy-start.3 = (bf16[1,2,8,16,512]{4,3,2,1,0:T(8,128)(2,1)S(1)}, bf16[1,2,8,16,512]{4,3,2,1,0:T(8,128)(2,1)}, u32[]{:S(2)}) copy-start(bf16[1,2,8,16,512]{4,3,2,1,0:T(8,128)(2,1)} %param.4) | copy-start | bytes 786436
  13.4 7.0 %collective-permute-start.2 = (bf16[1,2,8,16,512]{4,3,2,1,0:T(8,128)(2,1)S(1)}, bf16[1,2,8,16,512]{4,3,2,1,0:T(8,128)(2,1)S(1)}, u32[]{:S(2)}, u32[]{:S(2)}) collective-permute-start(bf16[1,2,8,16,512]{4,3,2,1,0:T(8,128)(2,1)S(1)} %collective-permute-done.1), channel_id=1, source_target_pairs={{0,2},{2,4},{4,6},{6,8},{8,10},{10,12},{12,14},{14,0},{1,3},{3,5},... | collective-permute-start | bytes 786440 | tf_op jit(solution)/shard_map/ppermute | solution.py:47
  17.3 15.9 %copy-start.1 = (bf16[1,2,8,144,512]{4,3,2,1,0:T(8,128)(2,1)}, bf16[1,2,8,144,512]{4,3,2,1,0:T(8,128)(2,1)S(1)}, u32[]{:S(2)}) copy-start(bf16[1,2,8,144,512]{4,3,2,1,0:T(8,128)(2,1)S(1)} %fusion.49) | copy-start | bytes 7077892
  17.3 8.0 %collective-permute-start.5 = (bf16[1,2,8,16,512]{4,3,2,1,0:T(8,128)(2,1)S(1)}, bf16[1,2,8,16,512]{4,3,2,1,0:T(8,128)(2,1)S(1)}, u32[]{:S(2)}, u32[]{:S(2)}) collective-permute-start(bf16[1,2,8,16,512]{4,3,2,1,0:T(8,128)(2,1)S(1)} %collective-permute-done.4), channel_id=1, source_target_pairs={{2,0},{4,2},{6,4},{8,6},{10,8},{12,10},{14,12},{0,14},{3,1},{5,3},... | collective-permute-start | bytes 786440 | tf_op jit(solution)/shard_map/ppermute | solution.py:49
  20.4 7.0 %collective-permute-start.3 = (bf16[1,2,8,16,512]{4,3,2,1,0:T(8,128)(2,1)S(1)}, bf16[1,2,8,16,512]{4,3,2,1,0:T(8,128)(2,1)S(1)}, u32[]{:S(2)}, u32[]{:S(2)}) collective-permute-start(bf16[1,2,8,16,512]{4,3,2,1,0:T(8,128)(2,1)S(1)} %collective-permute-done.2), channel_id=1, source_target_pairs={{0,2},{2,4},{4,6},{6,8},{8,10},{10,12},{12,14},{14,0},{1,3},{3,5},... | collective-permute-start | bytes 786440 | tf_op jit(solution)/shard_map/ppermute | solution.py:47
  25.3 7.2 %collective-permute-start.6 = (bf16[1,2,8,16,512]{4,3,2,1,0:T(8,128)(2,1)S(1)}, bf16[1,2,8,16,512]{4,3,2,1,0:T(8,128)(2,1)S(1)}, u32[]{:S(2)}, u32[]{:S(2)}) collective-permute-start(bf16[1,2,8,16,512]{4,3,2,1,0:T(8,128)(2,1)S(1)} %collective-permute-done.5), channel_id=1, source_target_pairs={{2,0},{4,2},{6,4},{8,6},{10,8},{12,10},{14,12},{0,14},{3,1},{5,3},... | collective-permute-start | bytes 786440 | tf_op jit(solution)/shard_map/ppermute | solution.py:49
  35.8 3.4 %copy-start.10 = (bf16[3,16,128]{2,1,0:T(8,128)(2,1)S(1)}, bf16[3,16,128]{2,1,0:T(8,128)(2,1)}, u32[]{:S(2)}) copy-start(bf16[3,16,128]{2,1,0:T(8,128)(2,1)} %get-tuple-element.30) | copy-start | bytes 36868
  36.1 24.3 %collective-permute-start.8 = (bf16[1,1,8,128,512]{4,3,2,1,0:T(8,128)(2,1)S(1)}, bf16[1,1,8,128,512]{4,3,2,1,0:T(8,128)(2,1)S(1)}, u32[]{:S(2)}, u32[]{:S(2)}) collective-permute-start(bf16[1,1,8,128,512]{4,3,2,1,0:T(8,128)(2,1)S(1)} %get-tuple-element.2), channel_id=1, source_target_pairs={{0,16},{16,32},{32,48},{48,64},{64,80},{80,96},{96,112},{112,128},... | collective-permute-start | bytes 3145736 | tf_op jit(solution)/shard_map/ppermute | solution.py:17
  38.0 26.5 %collective-permute-start.7 = (bf16[1,1,8,128,512]{4,3,2,1,0:T(8,128)(2,1)S(1)}, bf16[1,1,8,128,512]{4,3,2,1,0:T(8,128)(2,1)S(1)}, u32[]{:S(2)}, u32[]{:S(2)}) collective-permute-start(bf16[1,1,8,128,512]{4,3,2,1,0:T(8,128)(2,1)S(1)} %get-tuple-element.3), channel_id=1, source_target_pairs={{16,0},{32,16},{48,32},{64,48},{80,64},{96,80},{112,96},{128,112},... | collective-permute-start | bytes 3145736 | tf_op jit(solution)/shard_map/ppermute | solution.py:17
  39.7 0.7 copy-start.9
  39.8 1.0 copy-start.8
  41.3 1.7 %copy-start.2 = (bf16[1,2,8,144,512]{4,3,2,1,0:T(8,128)(2,1)S(1)}, bf16[1,2,8,144,512]{4,3,2,1,0:T(8,128)(2,1)}, u32[]{:S(2)}) copy-start(bf16[1,2,8,144,512]{4,3,2,1,0:T(8,128)(2,1)} %copy-done.1) | copy-start | bytes 7077892
  61.1 5.5 %copy-start.7 = (bf16[3,16,128]{2,1,0:T(8,128)(2,1)S(1)}, bf16[3,16,128]{2,1,0:T(8,128)(2,1)}, u32[]{:S(2)}) copy-start(bf16[3,16,128]{2,1,0:T(8,128)(2,1)} %get-tuple-element.34) | copy-start | bytes 36868
  65.3 1.8 %copy-start.6 = (bf16[3,16,128]{2,1,0:T(8,128)(2,1)S(1)}, bf16[3,16,128]{2,1,0:T(8,128)(2,1)}, u32[]{:S(2)}) copy-start(bf16[3,16,128]{2,1,0:T(8,128)(2,1)} %get-tuple-element.28) | copy-start | bytes 36868
  65.3 6.7 %collective-permute-start.9 = (f32[27,16,128]{2,1,0:T(8,128)S(1)}, f32[27,16,128]{2,1,0:T(8,128)S(1)}, u32[]{:S(2)}, u32[]{:S(2)}) collective-permute-start(f32[27,16,128]{2,1,0:T(8,128)S(1)} %bitcast.190), channel_id=1, source_target_pairs={{0,1},{1,0},{2,3},{3,2},{4,5},{5,4},{6,7},{7,6},{8,9},{9,8},{10,11... | collective-permute-start | bytes 663560 | tf_op jit(solution)/shard_map/ppermute | solution.py:22
  67.5 0.7 copy-start.5
  72.1 6.2 %collective-permute-start.10 = (f32[27,16,128]{2,1,0:T(8,128)S(1)}, f32[27,16,128]{2,1,0:T(8,128)S(1)}, u32[]{:S(2)}, u32[]{:S(2)}) collective-permute-start(f32[27,16,128]{2,1,0:T(8,128)S(1)} %add.209), channel_id=1, source_target_pairs={{0,16},{16,0},{32,48},{48,32},{64,80},{80,64},{96,112},{112,96},{1... | collective-permute-start | bytes 663560 | tf_op jit(solution)/shard_map/ppermute | solution.py:22
  78.4 10.5 %collective-permute-start.11 = (f32[27,16,128]{2,1,0:T(8,128)S(1)}, f32[27,16,128]{2,1,0:T(8,128)S(1)}, u32[]{:S(2)}, u32[]{:S(2)}) collective-permute-start(f32[27,16,128]{2,1,0:T(8,128)S(1)} %add.210), channel_id=1, source_target_pairs={{0,128},{16,144},{32,160},{48,176},{64,192},{80,208},{96,224},{112... | collective-permute-start | bytes 663560 | tf_op jit(solution)/shard_map/ppermute | solution.py:22
  88.9 12.8 %collective-permute-start.12 = (f32[27,16,128]{2,1,0:T(8,128)S(1)}, f32[27,16,128]{2,1,0:T(8,128)S(1)}, u32[]{:S(2)}, u32[]{:S(2)}) collective-permute-start(f32[27,16,128]{2,1,0:T(8,128)S(1)} %add.211), channel_id=1, source_target_pairs={{0,32},{16,48},{32,0},{48,16},{64,96},{80,112},{96,64},{112,80},{1... | collective-permute-start | bytes 663560 | tf_op jit(solution)/shard_map/ppermute | solution.py:22
  101.7 16.1 %collective-permute-start.13 = (f32[27,16,128]{2,1,0:T(8,128)S(1)}, f32[27,16,128]{2,1,0:T(8,128)S(1)}, u32[]{:S(2)}, u32[]{:S(2)}) collective-permute-start(f32[27,16,128]{2,1,0:T(8,128)S(1)} %add.212), channel_id=1, source_target_pairs={{0,64},{16,80},{32,96},{48,112},{64,0},{80,16},{96,32},{112,48},{1... | collective-permute-start | bytes 663560 | tf_op jit(solution)/shard_map/ppermute | solution.py:22
